TPU v7x, 32 devices: a whole 2x2x4 slice. The times are simulated.
32 devices in a mesh: grp: 4 (over z), ep: 8 (over y, x, core).
Axes of the slice: x: 2, y: 2, z: 4, core: 2. Of those that a mesh axis runs over, the one named last changes fastest.
Arguments:
- resid: bfloat16 [8, 512, 2304], P('ep', 'grp'), may hold values from -6 to 6
- queries: bfloat16 [8, 512, 2304], P('ep', 'grp'), may hold values from -6 to 6
- keys: bfloat16 [8, 512, 2304], P('ep', 'grp'), may hold values from -6 to 6
- values: bfloat16 [8, 512, 2304], P('ep', 'grp'), may hold values from -6 to 6
- tenant: int32 [8, 512], P('ep', 'grp'), may hold values from 0 to 3, never falling along the last dimension, each value on 1 to 256 neighbouring positions
- out_proj: bfloat16 [2304, 2304], replicated, may hold values from -0.125 to 0.125
- norm_gain: float32 [2304], replicated, may hold values from 0.1 to 1.9
- router: bfloat16 [2304, 8], replicated, may hold values from -0.125 to 0.125
- routes: int32 [8, 512, 2], P('ep', 'grp'), may hold values from 0 to 7, all different within a row; in each aligned block of 128 rows (0 to 127, 128 to 255, ..., all dimensions but the last counted through in order) at most 40 rows name the same one
- expert_in: bfloat16 [8, 2304, 2, 5760], P('ep', None, None, 'grp'), as said below
- expert_out: bfloat16 [8, 5760, 2304], P('ep', 'grp'), as said below
Outputs:
- layer_out: bfloat16 [8, 512, 2304], P('ep', 'grp')
Inputs may be any that keep to these rules, and one draw needn't show every extreme that they name: Within each sequence tenant ids never fall; one tenant range spans exactly 256 positions. `routes`: the two experts of a token differ; in each aligned block of 128 tokens of one device no expert is named by more than 40 tokens, and some block names some expert exactly 40 times. `expert_in`: entries j and k with j == k // 1 are equal. `expert_out`: entries j and k with j == k // 1 are equal.
All inputs are finite; a program needn't handle non-finite values.
Results may differ from a plain program's by a relative error of at most 0.0056.
Values may be sent and summed in bfloat16 or wider, within the bound.
No kernel may reach another device: no remote copies, remote signals or barrier semaphores. Data moves between devices by JAX's collectives and lax.ppermute only.
A program may use at most 192 MiB of HBM per device.

v0:
```python
import jax
import jax.numpy as jnp
from jax import lax
from jax.sharding import PartitionSpec as P

HEADS = 36
HEAD_DIM = 64
EXPERTS = 8
TOP = 2


NEG = -1e30


def local(
    resid, queries, keys, values, tenant, out_proj, norm_gain, router, routes, expert_in, expert_out
):
    rows_here = resid.shape[1]
    width = resid.shape[2]
    n_ep = lax.axis_size("ep")
    n_grp = lax.axis_size("grp")
    replicas = n_ep // EXPERTS
    block = rows_here // replicas
    capacity = block * 5 // 16
    offset = lax.axis_index("grp") * rows_here
    query_heads = queries[0].reshape(rows_here, HEADS, HEAD_DIM)
    query_pos = offset + jnp.arange(rows_here, dtype=jnp.int32)
    query_seg = tenant[0].astype(jnp.bfloat16)
    scale = HEAD_DIM ** (-0.5)
    seg_wire = tenant.astype(jnp.bfloat16)
    running = jnp.full((HEADS, rows_here), NEG, jnp.float32)
    key_piece = lax.all_gather(keys, "grp", axis=1, tiled=True)
    value_piece = lax.all_gather(values, "grp", axis=1, tiled=True)
    seg_piece = lax.all_gather(seg_wire, "grp", axis=1, tiled=True)
    count = key_piece.shape[1]
    key_heads = key_piece[0].reshape(count, HEADS, HEAD_DIM)
    value_heads = value_piece[0].reshape(count, HEADS, HEAD_DIM)
    scores = (
        jnp.einsum("qhd,khd->hqk", query_heads, key_heads, preferred_element_type=jnp.float32)
        * scale
    )
    key_pos = jnp.arange(count, dtype=jnp.int32)
    allowed = (query_pos[:, None] >= key_pos[None, :]) & (
        query_seg[:, None] == seg_piece[0][None, :]
    )
    scores = jnp.where(allowed[None], scores, NEG)
    newest = jnp.maximum(running, jnp.max(scores, axis=-1))
    probs = jnp.where(allowed[None], jnp.exp(scores - newest[..., None]), 0.0)
    total = jnp.sum(probs, axis=-1)
    accum = jnp.einsum(
        "hqk,khd->hqd", probs.astype(jnp.bfloat16), value_heads, preferred_element_type=jnp.float32
    )
    running, total, accum = (newest, total, accum)
    attended = (
        jnp.transpose(accum / total[..., None], (1, 0, 2))
        .reshape(rows_here, width)
        .astype(jnp.bfloat16)
    )
    residual = resid[0].astype(jnp.float32) + jnp.dot(
        attended, out_proj, preferred_element_type=jnp.float32
    )
    normed = (
        residual
        * lax.rsqrt(jnp.mean(residual * residual, axis=-1, keepdims=True) + 1e-05)
        * norm_gain
    ).astype(jnp.bfloat16)
    logits = jnp.dot(normed, router, preferred_element_type=jnp.float32)
    local_routes = routes[0]
    expert_ids = jnp.arange(EXPERTS, dtype=jnp.int32)
    picked = jnp.sum(
        jnp.where(local_routes[:, :, None] == expert_ids[None, None, :], logits[:, None, :], 0.0),
        axis=-1,
    )
    gate_weights = jax.nn.softmax(picked, axis=-1).astype(jnp.bfloat16)
    half_id = jnp.arange(rows_here, dtype=jnp.int32) // block
    destination = local_routes * replicas + half_id[:, None]
    flat_dest = destination.reshape(-1)
    onehot = (flat_dest[:, None] == jnp.arange(n_ep, dtype=jnp.int32)[None, :]).astype(jnp.int32)
    earlier = jnp.cumsum(onehot, axis=0) - onehot
    position = jnp.sum(earlier * onehot, axis=1)
    slot = (flat_dest * capacity + position).reshape(rows_here, TOP)
    n_slots = n_ep * capacity
    matches = jnp.arange(n_slots, dtype=jnp.int32)[:, None, None] == slot[None]
    dispatch_table = jnp.any(matches, axis=-1).astype(jnp.bfloat16)
    outgoing = jnp.dot(dispatch_table, normed, preferred_element_type=jnp.float32).astype(
        jnp.bfloat16
    )
    outgoing = outgoing.reshape(n_ep, capacity, width)
    combine = jnp.transpose(
        jnp.sum(jnp.where(matches, gate_weights.astype(jnp.float32)[None], 0.0), axis=-1)
    ).astype(jnp.bfloat16)
    weight_in = expert_in[0]
    weight_out = expert_out[0]
    ff_here = weight_in.shape[2]
    weight_matrix = weight_in.reshape(width, 2 * ff_here)
    copies = jnp.broadcast_to(outgoing[None], (n_grp, n_ep, capacity, width)).reshape(
        n_grp * n_ep, capacity, width
    )
    arrived = lax.all_to_all(
        copies, ("grp", "ep"), split_axis=0, concat_axis=0, tiled=True
    ).reshape(n_grp * n_slots, width)
    both = jnp.dot(arrived, weight_matrix, preferred_element_type=jnp.float32)
    hidden = (jax.nn.silu(both[:, :ff_here]) * both[:, ff_here:]).astype(jnp.bfloat16)
    partial_value = (
        jnp.dot(hidden, weight_out, preferred_element_type=jnp.float32)
        .astype(jnp.bfloat16)
        .reshape(n_grp * n_ep, capacity, width)
    )
    returned = lax.all_to_all(partial_value, ("grp", "ep"), split_axis=0, concat_axis=0, tiled=True)
    summed = jnp.sum(returned.reshape(n_grp, n_slots, width).astype(jnp.float32), axis=0).astype(
        jnp.bfloat16
    )
    moe = jnp.dot(combine, summed, preferred_element_type=jnp.float32)
    return (residual + moe).astype(jnp.bfloat16)[None]


def solution(mesh):
    in_specs = (
        P("ep", "grp", None),
        P("ep", "grp", None),
        P("ep", "grp", None),
        P("ep", "grp", None),
        P("ep", "grp"),
        P(),
        P(),
        P(),
        P("ep", "grp", None),
        P("ep", None, None, "grp"),
        P("ep", "grp", None),
    )
    out_specs = P("ep", "grp", None)
    return jax.shard_map(local, mesh=mesh, in_specs=in_specs, out_specs=out_specs, check_vma=False)
```

profile of v0, /device:TPU:0, one launch (start us, length us, event | category | flops | bytes accessed | tf_op | source)
XLA Modules:
  0.0 444.5 jit_solution(8121430287009658407)
XLA Ops:
  6.5 0.7 all-gather.3.cloned.1.call-update
  7.3 0.7 all-gather.5.cloned.1.call-update
  8.0 0.8 copy.40
  9.1 1.4 copy.37
  12.1 0.7 convert_bitcast_fusion
  12.8 12.6 %all_gather.11 = bf16[1,512]{1,0:T(2,128)(2,1)S(1)} all-gather(bf16[1,128]{1,0:T(2,128)(2,1)S(1)} %get-tuple-element.6), channel_id=1, replica_groups=mesh['grp'=4,'ep'=8] {'grp'}, dimensions={1}, use_global_device_ids=true | all-gather | bytes 1280 | tf_op jit(solution)/shard_map/all_gather | solution.py:34
  25.4 0.7 add_bitcast_fusion
  26.3 35.9 %all-gather.3.cloned.1.call-done = bf16[1,512,2304]{2,1,0:T(8,128)(2,1)} async-done(((bf16[1,128,2304]{2,1,0:T(8,128)(2,1)}), bf16[1,512,2304]{2,1,0:T(8,128)(2,1)}) %all-gather.3.cloned.1.call-update) | async-done | bytes 2359312 | tf_op jit(solution)/shard_map/all_gather | solution.py:32
  62.2 2.8 copy.38
  65.0 2.0 fusion
  67.0 3.6 copy-done.1
  70.6 2.9 fusion.2
  73.5 39.5 %all-gather.5.cloned.1.call-done = bf16[1,512,2304]{2,1,0:T(8,128)(2,1)} async-done(((bf16[1,128,2304]{2,1,0:T(8,128)(2,1)}), bf16[1,512,2304]{2,1,0:T(8,128)(2,1)}) %all-gather.5.cloned.1.call-update) | async-done | bytes 2359312 | tf_op jit(solution)/shard_map/all_gather | solution.py:33
  113.0 4.4 copy.39
  117.5 7.2 %divide_convert_fusion = bf16[128,36,64]{0,2,1:T(8,128)(2,1)S(1)} fusion(bf16[512,36,64]{0,2,1:T(8,128)(2,1)} %bitcast.57, f32[36,128,512]{2,1,0:T(8,128)} %copy-done.1, f32[36,128]{1,0:T(8,128)S(1)} %broadcast_maximum_fusion, pred[128,512]{1,0:T(8,128)(4,1)S(1)} %fusion.18, f32[128,36]{0,1:T(8,128)S(1)} %bitcast.59), kind=kOutput, calls=%fused_computation.21 | convolution fusion | flops 314376192 | bytes 12488704 | tf_op jit(solution)/shard_map/hqk,khd->hqd/dot_general | solution.py:50
  124.7 1.7 multiply_reduce_fusion
  126.5 0.6 convolution_convert_fusion.1
  127.5 133.5 %all_to_all.10 = bf16[32,40,2304]{2,1,0:T(8,128)(2,1)S(1)} all-to-all(bf16[32,40,2304]{2,1,0:T(8,128)(2,1)S(1)} %bitcast.49), channel_id=1, replica_groups=mesh['grp'=4,'ep'=8] {'grp','ep'}, dimensions={0} | all-to-all | bytes 11796480 | tf_op jit(solution)/shard_map/all_to_all | solution.py:99
  261.0 21.9 %fusion.30 = f32[1280,2880]{0,1:T(8,128)} fusion(bf16[1280,2304]{1,0:T(8,128)(2,1)S(1)} %bitcast.55, bf16[2304,2880]{0,1:T(8,128)(2,1)} %bitcast.61), kind=kOutput, calls=%fused_computation.56 | convolution fusion | flops 16986931200 | bytes 33914880 | tf_op jit(solution)/shard_map/dot_general | solution.py:102
  282.9 14.9 %convolution_convert_fusion = bf16[1280,2304]{1,0:T(8,128)(2,1)} fusion(bf16[1,1440,2304]{2,1,0:T(8,128)(2,1)S(1)} %bitcast.63, f32[1280,2880]{0,1:T(8,128)} %fusion.30), kind=kOutput, calls=%fused_computation | convolution fusion | flops 8507473920 | bytes 27279360 | tf_op jit(solution)/shard_map/dot_general | solution.py:105
  297.8 3.8 all-to-all-start.1
  302.1 130.8 %all-to-all-done.1 = bf16[32,40,2304]{2,1,0:T(8,128)(2,1)} async-done(((bf16[32,40,2304]{2,1,0:T(8,128)(2,1)}), bf16[32,40,2304]{2,1,0:T(8,128)(2,1)}, u32[]{:S(2)}, u32[]{:S(2)}) %all-to-all-start.1) | async-done | bytes 5898272 | tf_op jit(solution)/shard_map/all_to_all | solution.py:109
  432.9 3.5 bitcast_reduce_fusion
  436.4 1.3 fusion.11
  (54 shorter events, 3.0 us)
Async XLA Ops:
  6.5 295.1 %copy-start = (bf16[2304,8]{0,1:T(8,128)(2,1)S(1)}, bf16[2304,8]{0,1:T(8,128)(2,1)}, u32[]{:S(2)}) copy-start(bf16[2304,8]{0,1:T(8,128)(2,1)} %param.18) | copy-start | bytes 110596
  6.5 55.6 %all-gather.3.cloned.1.call-start = ((), (), s32[]{:S(2)}) async-start(), calls=%async_computation.2 | async-start | bytes 2949120 | tf_op jit(solution)/shard_map/all_gather | solution.py:32
  7.3 105.8 %all-gather.5.cloned.1.call-start = ((), (), s32[]{:S(2)}) async-start(), calls=%async_computation.3 | async-start | bytes 2949120 | tf_op jit(solution)/shard_map/all_gather | solution.py:33
  67.0 3.6 copy-start.1
  113.0 11.6 %slice-start = ((s8[10616832]{0:T(1024)(128)(4,1)}), s8[2228224]{0:T(1024)(128)(4,1)S(1)}, s32[]{:S(2)}) async-start(s8[10616832]{0:T(1024)(128)(4,1)} %bitcast.50), calls=%async_computation.4 | async-start | bytes 4456448
  117.5 7.2 %slice-start.1 = ((s8[10616832]{0:T(1024)(128)(4,1)}), s8[4194304]{0:T(1024)(128)(4,1)S(1)}, s32[]{:S(2)}) async-start(s8[10616832]{0:T(1024)(128)(4,1)} %bitcast.50), calls=%async_computation.5 | async-start | bytes 8388608
  117.5 7.2 %slice-start.2 = ((s8[10616832]{0:T(1024)(128)(4,1)}), s8[4194304]{0:T(1024)(128)(4,1)S(1)}, s32[]{:S(2)}) async-start(s8[10616832]{0:T(1024)(128)(4,1)} %bitcast.50), calls=%async_computation.6 | async-start | bytes 8388608
  117.5 7.2 %copy-start.2 = (bf16[1,128,2304]{2,1,0:T(8,128)(2,1)S(1)}, bf16[1,128,2304]{2,1,0:T(8,128)(2,1)}, u32[]{:S(2)}) copy-start(bf16[1,128,2304]{2,1,0:T(8,128)(2,1)} %param.11) | copy-start | bytes 1769476
  124.7 1.8 copy-start.3
  127.5 155.4 %slice-start.3 = ((s8[6635520]{0:T(1024)(128)(4,1)}), s8[4194304]{0:T(1024)(128)(4,1)S(1)}, s32[]{:S(2)}) async-start(s8[6635520]{0:T(1024)(128)(4,1)} %bitcast.62), calls=%async_computation.7 | async-start | bytes 8388608
  261.0 21.9 %slice-start.4 = ((s8[6635520]{0:T(1024)(128)(4,1)}), s8[2441216]{0:T(1024)(128)(4,1)S(1)}, s32[]{:S(2)}) async-start(s8[6635520]{0:T(1024)(128)(4,1)} %bitcast.62), calls=%async_computation.8 | async-start | bytes 4882432
  297.8 4.1 copy-start.4
  297.8 135.1 %all-to-all-start.1 = ((bf16[32,40,2304]{2,1,0:T(8,128)(2,1)}), bf16[32,40,2304]{2,1,0:T(8,128)(2,1)}, u32[]{:S(2)}, u32[]{:S(2)}) async-start(bf16[32,40,2304]{2,1,0:T(8,128)(2,1)} %bitcast.54), calls=%async_computation.1 | async-start | bytes 11796480 | tf_op jit(solution)/shard_map/all_to_all | solution.py:109
Sparse Core Ops, SparseCore 0:
  8.9 53.1 all-gather.2
  63.7 49.2 all-gather.4
where the time goes:
time: 445 us
  waiting for transfers between devices  208 us (47%)
  blocking collectives  146 us (33%)
  matrix products  50 us (11%)
  local copies, waits for them, and re-layouts  14.6 us (3%)
  between operations  13.6 us (3%)
  other arithmetic  8.81 us (2%)
    all_to_all x1, blocking collectives, local(): lax.all_to_all(copies, ('grp', 'ep'), split_axis=0, concat_axis=0, tiled=...  133 us
    all_to_all x1, waiting for transfers between devices, local(): lax.all_to_all(partial_value, ('grp', 'ep'), split_axis=0, concat_axis=0,...  131 us
    all_gather x1, waiting for transfers between devices, local(): value_piece = lax.all_gather(values, 'grp', axis=1, tiled=True)  39.5 us
    all_gather x1, waiting for transfers between devices, local(): key_piece = lax.all_gather(keys, 'grp', axis=1, tiled=True)  35.9 us
    dot_general x1, matrix products, local(): both = jnp.dot(arrived, weight_matrix, preferred_element_type=jnp.float32)  21.9 us
    dot_general x1, matrix products, local(): jnp.dot(hidden, weight_out, preferred_element_type=jnp.float32)  14.9 us
    all_gather x1, blocking collectives, local(): seg_piece = lax.all_gather(seg_wire, 'grp', axis=1, tiled=True)  12.6 us
  transfers between devices with their start and end apart: 3, of which 3 were waited for; matrix products, arithmetic and copies ran while one was open for 3% of the time, Pallas kernels for 0%

commit v1 on v0

--- a/solution.py
+++ b/solution.py
@@ -12,6 +12,10 @@
 NEG = -1e30
 
 
+def shift_up(x, n_grp):
+    return lax.ppermute(x, "grp", perm=[(i, i + 1) for i in range(n_grp - 1)])
+
+
 def local(
     resid, queries, keys, values, tenant, out_proj, norm_gain, router, routes, expert_in, expert_out
 ):
@@ -19,38 +23,54 @@
     width = resid.shape[2]
     n_ep = lax.axis_size("ep")
     n_grp = lax.axis_size("grp")
+    seq_len = rows_here * n_grp
     replicas = n_ep // EXPERTS
     block = rows_here // replicas
     capacity = block * 5 // 16
-    offset = lax.axis_index("grp") * rows_here
+    me_grp = lax.axis_index("grp")
+    offset = me_grp * rows_here
+    span = seq_len // 2
+    back = min(n_grp - 1, -(-(span - 1) // rows_here))
+
     query_heads = queries[0].reshape(rows_here, HEADS, HEAD_DIM)
     query_pos = offset + jnp.arange(rows_here, dtype=jnp.int32)
-    query_seg = tenant[0].astype(jnp.bfloat16)
+    query_seg = tenant[0]
     scale = HEAD_DIM ** (-0.5)
-    seg_wire = tenant.astype(jnp.bfloat16)
-    running = jnp.full((HEADS, rows_here), NEG, jnp.float32)
-    key_piece = lax.all_gather(keys, "grp", axis=1, tiled=True)
-    value_piece = lax.all_gather(values, "grp", axis=1, tiled=True)
-    seg_piece = lax.all_gather(seg_wire, "grp", axis=1, tiled=True)
-    count = key_piece.shape[1]
-    key_heads = key_piece[0].reshape(count, HEADS, HEAD_DIM)
-    value_heads = value_piece[0].reshape(count, HEADS, HEAD_DIM)
+
+    key_chunks = [keys[0]]
+    value_chunks = [values[0]]
+    seg_chunks = [tenant[0]]
+    k_cur, v_cur, s_cur = keys[0], values[0], tenant[0]
+    for _ in range(back):
+        k_cur = shift_up(k_cur, n_grp)
+        v_cur = shift_up(v_cur, n_grp)
+        s_cur = shift_up(s_cur, n_grp)
+        key_chunks.insert(0, k_cur)
+        value_chunks.insert(0, v_cur)
+        seg_chunks.insert(0, s_cur)
+    key_piece = jnp.concatenate(key_chunks, axis=0)
+    value_piece = jnp.concatenate(value_chunks, axis=0)
+    seg_piece = jnp.concatenate(seg_chunks, axis=0)
+    count = key_piece.shape[0]
+    key_pos = offset - back * rows_here + jnp.arange(count, dtype=jnp.int32)
+    key_heads = key_piece.reshape(count, HEADS, HEAD_DIM)
+    value_heads = value_piece.reshape(count, HEADS, HEAD_DIM)
     scores = (
         jnp.einsum("qhd,khd->hqk", query_heads, key_heads, preferred_element_type=jnp.float32)
         * scale
     )
-    key_pos = jnp.arange(count, dtype=jnp.int32)
-    allowed = (query_pos[:, None] >= key_pos[None, :]) & (
-        query_seg[:, None] == seg_piece[0][None, :]
+    allowed = (
+        (query_pos[:, None] >= key_pos[None, :])
+        & (key_pos[None, :] >= 0)
+        & (query_seg[:, None] == seg_piece[None, :])
     )
     scores = jnp.where(allowed[None], scores, NEG)
-    newest = jnp.maximum(running, jnp.max(scores, axis=-1))
+    newest = jnp.max(scores, axis=-1)
     probs = jnp.where(allowed[None], jnp.exp(scores - newest[..., None]), 0.0)
     total = jnp.sum(probs, axis=-1)
     accum = jnp.einsum(
         "hqk,khd->hqd", probs.astype(jnp.bfloat16), value_heads, preferred_element_type=jnp.float32
     )
-    running, total, accum = (newest, total, accum)
     attended = (
         jnp.transpose(accum / total[..., None], (1, 0, 2))
         .reshape(rows_here, width)
@@ -93,22 +113,21 @@
     weight_out = expert_out[0]
     ff_here = weight_in.shape[2]
     weight_matrix = weight_in.reshape(width, 2 * ff_here)
-    copies = jnp.broadcast_to(outgoing[None], (n_grp, n_ep, capacity, width)).reshape(
-        n_grp * n_ep, capacity, width
+    in_plane = lax.all_to_all(outgoing, "ep", split_axis=0, concat_axis=0, tiled=True)
+    arrived = lax.all_gather(in_plane, "grp", axis=0, tiled=False).reshape(
+        n_grp * n_slots, width
     )
-    arrived = lax.all_to_all(
-        copies, ("grp", "ep"), split_axis=0, concat_axis=0, tiled=True
-    ).reshape(n_grp * n_slots, width)
     both = jnp.dot(arrived, weight_matrix, preferred_element_type=jnp.float32)
     hidden = (jax.nn.silu(both[:, :ff_here]) * both[:, ff_here:]).astype(jnp.bfloat16)
     partial_value = (
         jnp.dot(hidden, weight_out, preferred_element_type=jnp.float32)
         .astype(jnp.bfloat16)
-        .reshape(n_grp * n_ep, capacity, width)
+        .reshape(n_grp, n_ep, capacity, width)
     )
-    returned = lax.all_to_all(partial_value, ("grp", "ep"), split_axis=0, concat_axis=0, tiled=True)
-    summed = jnp.sum(returned.reshape(n_grp, n_slots, width).astype(jnp.float32), axis=0).astype(
-        jnp.bfloat16
+    slices = lax.all_to_all(partial_value, "grp", split_axis=0, concat_axis=0, tiled=True)
+    expert_output = jnp.sum(slices.astype(jnp.float32), axis=0).astype(jnp.bfloat16)
+    summed = lax.all_to_all(expert_output, "ep", split_axis=0, concat_axis=0, tiled=True).reshape(
+        n_slots, width
     )
     moe = jnp.dot(combine, summed, preferred_element_type=jnp.float32)
     return (residual + moe).astype(jnp.bfloat16)[None]

time: 445 us -> 421 us (0.946)
  waiting for transfers between devices: 208 us -> 148 us
  starting transfers between devices: 3.8 us -> 28.9 us
  blocking collectives: 146 us -> 157 us
    all_to_all x1, waiting for transfers between devices: 131 us -> 19.5 us  [local(): lax.all_to_all(expert_output, 'ep', split_axis=0, concat_axis=0, tiled=True)]
    all_gather x2 -> x1, waiting for transfers between devices: 75.4 us -> 109 us  [local(): lax.all_gather(in_plane, 'grp', axis=0, tiled=False)]
    ppermute x0 -> x6, starting transfers between devices: none -> 25.1 us  [shift_up(): return lax.ppermute(x, 'grp', perm=[(i, i + 1) for i in range(n_grp - 1)])]
    all_to_all x1 -> x2, blocking collectives: 133 us -> 157 us  [the longest x1 134 us: local(): lax.all_to_all(partial_value, 'grp', split_axis=0, concat_axis=0, tiled=T...]
    ppermute x0 -> x6, waiting for transfers between devices: none -> 19 us  [shift_up(): return lax.ppermute(x, 'grp', perm=[(i, i + 1) for i in range(n_grp - 1)])]
    all_gather x1 -> x0, blocking collectives: 12.6 us -> none  [local(): seg_piece = lax.all_gather(seg_wire, 'grp', axis=1, tiled=True)]
    all_gather x2 -> x0, local copies, waits for them, and re-layouts: 7.26 us -> none  [the longest x1 4.42 us: local(): value_piece = lax.all_gather(values, 'grp', axis=1, tiled=True)]
  transfers between devices with their start and end apart: 3 -> 8, of which waited for: 3 -> 5; matrix products, arithmetic and copies ran while one was open for 3% -> 4% of each run, Pallas kernels for 0% -> 0%
where the time goes in v1:
time: 421 us; the launch traced here: 420 us
  blocking collectives  157 us (37%)
  waiting for transfers between devices  148 us (35%)
  matrix products  50.5 us (12%)
  starting transfers between devices  28.9 us (7%)
  between operations  13.7 us (3%)
  other arithmetic  11.2 us (3%)
  local copies, waits for them, and re-layouts  10.9 us (3%)
    all_to_all x1, blocking collectives, local(): lax.all_to_all(partial_value, 'grp', split_axis=0, concat_axis=0, tiled=T...  134 us
    all_gather x1, waiting for transfers between devices, local(): lax.all_gather(in_plane, 'grp', axis=0, tiled=False)  109 us
    ppermute x6, starting transfers between devices, shift_up(): return lax.ppermute(x, 'grp', perm=[(i, i + 1) for i in range(n_grp - 1)])  25.1 us
    all_to_all x1, blocking collectives, local(): lax.all_to_all(outgoing, 'ep', split_axis=0, concat_axis=0, tiled=True)  23.5 us
    dot_general x1, matrix products, local(): both = jnp.dot(arrived, weight_matrix, preferred_element_type=jnp.float32)  23.5 us
    all_to_all x1, waiting for transfers between devices, local(): lax.all_to_all(expert_output, 'ep', split_axis=0, concat_axis=0, tiled=True)  19.5 us
    ppermute x6, waiting for transfers between devices, shift_up(): return lax.ppermute(x, 'grp', perm=[(i, i + 1) for i in range(n_grp - 1)])  19 us
    dot_general x1, matrix products, local(): jnp.dot(hidden, weight_out, preferred_element_type=jnp.float32)  14.9 us
  transfers between devices with their start and end apart: 8, of which 5 were waited for; matrix products, arithmetic and copies ran while one was open for 4% of the time, Pallas kernels for 0%

profile of v1, /device:TPU:0, one launch (start us, length us, event | category | flops | bytes accessed | tf_op | source)
XLA Modules:
  0.0 420.4 jit_solution(13155206042010199163)
XLA Ops:
  6.5 5.1 %collective-permute-start.2 = (bf16[128,2304]{1,0:T(8,128)(2,1)}, bf16[128,2304]{1,0:T(8,128)(2,1)S(1)}, u32[]{:S(2)}, u32[]{:S(2)}) collective-permute-start(bf16[128,2304]{1,0:T(8,128)(2,1)} %bitcast.69), channel_id=1, source_target_pairs={{0,8},{8,16},{16,24},{1,9},{9,17},{17,25},{2,10},{10,18},{18,26},{... | collective-permute-start | bytes 1769480 | tf_op jit(solution)/shard_map/ppermute | solution.py:16
  11.6 3.4 collective-permute-start
  15.1 3.5 collective-permute-start.4
  22.1 3.5 collective-permute-done.2
  25.6 5.1 %collective-permute-start.3 = (bf16[128,2304]{1,0:T(8,128)(2,1)S(1)}, bf16[128,2304]{1,0:T(8,128)(2,1)}, u32[]{:S(2)}, u32[]{:S(2)}) collective-permute-start(bf16[128,2304]{1,0:T(8,128)(2,1)S(1)} %collective-permute-done.2), channel_id=1, source_target_pairs={{0,8},{8,16},{16,24},{1,9},{9,17},{17,25},{2,10},{10,18},{18,26},{... | collective-permute-start | bytes 1769480 | tf_op jit(solution)/shard_map/ppermute | solution.py:16
  30.7 2.7 collective-permute-start.1
  33.5 1.4 copy.69
  34.8 2.1 copy.73
  36.9 1.4 copy.70
  38.3 11.4 %collective-permute-done.1 = s32[128]{0:T(128)S(1)} collective-permute-done((s32[128]{0:T(128)S(1)}, s32[128]{0:T(128)S(1)}, u32[]{:S(2)}, u32[]{:S(2)}) %collective-permute-start.1) | collective-permute-done | bytes 544 | tf_op jit(solution)/shard_map/ppermute | solution.py:16
  51.3 5.3 %collective-permute-start.5 = (bf16[128,2304]{1,0:T(8,128)(2,1)S(1)}, bf16[128,2304]{1,0:T(8,128)(2,1)}, u32[]{:S(2)}, u32[]{:S(2)}) collective-permute-start(bf16[128,2304]{1,0:T(8,128)(2,1)S(1)} %collective-permute-done.4), channel_id=1, source_target_pairs={{0,8},{8,16},{16,24},{1,9},{9,17},{17,25},{2,10},{10,18},{18,26},{... | collective-permute-start | bytes 1769480 | tf_op jit(solution)/shard_map/ppermute | solution.py:16
  56.6 1.4 copy.67
  59.2 4.2 %fusion.46 = (f32[36,128]{1,0:T(8,128)S(1)}, bf16[36,128,384]{1,2,0:T(8,128)(2,1)}) fusion(f32[36,384,128]{2,1,0:T(8,128)S(1)} %fusion.18, pred[128,384]{0,1:T(8,128)(4,1)S(1)} %compare_and_fusion), kind=kOutput, calls=%fused_computation.69 | output fusion | flops 14156159 | bytes 10684416 | tf_op jit(solution)/shard_map/sub | solution.py:69
  63.4 4.1 collective-permute-done.5
  68.9 2.9 divide_convert_fusion
  71.8 5.7 %multiply_reduce_fusion = (f32[128]{0:T(128)S(1)}, f32[128,2304]{1,0:T(8,128)S(1)}) fusion(bf16[128,2304]{0,1:T(8,128)(2,1)S(1)} %bitcast.68, bf16[2304,2304]{1,0:T(8,128)(2,1)} %param.16, bf16[1,128,2304]{2,1,0:T(8,128)(2,1)S(1)} %copy-done.3), kind=kOutput, calls=%fused_computation.32 | convolution fusion | flops 1360134016 | bytes 12976640 | tf_op jit(solution)/shard_map/dot_general | solution.py:79
  78.2 23.5 %all_to_all.15 = bf16[8,40,2304]{2,1,0:T(8,128)(2,1)} all-to-all(bf16[8,40,2304]{2,1,0:T(8,128)(2,1)S(1)} %bitcast.63), channel_id=1, replica_groups=mesh['grp'=4,'ep'=8] {'ep'}, dimensions={0} | all-to-all | bytes 2949120 | tf_op jit(solution)/shard_map/all_to_all | solution.py:116
  101.8 109.4 %all-gather.3.cloned.1.call-done = bf16[32,40,2304]{2,1,0:T(8,128)(2,1)} async-done(((bf16[8,40,2304]{2,1,0:T(8,128)(2,1)}), bf16[32,40,2304]{2,1,0:T(8,128)(2,1)}) %all-gather.3.cloned.1.call-update) | async-done | bytes 5898256 | tf_op jit(solution)/shard_map/all_gather | solution.py:117
  211.2 23.5 %fusion.47 = f32[1280,2880]{0,1:T(8,128)} fusion(bf16[1280,2304]{1,0:T(8,128)(2,1)} %bitcast.79, bf16[2304,2880]{0,1:T(8,128)(2,1)} %bitcast.78), kind=kOutput, calls=%fused_computation.70 | convolution fusion | flops 16986931200 | bytes 33914880 | tf_op jit(solution)/shard_map/dot_general | solution.py:120
  234.7 14.9 %convolution_convert_fusion = bf16[1280,2304]{1,0:T(8,128)(2,1)S(1)} fusion(bf16[1,1440,2304]{2,1,0:T(8,128)(2,1)} %param.21, f32[1280,2880]{0,1:T(8,128)} %fusion.47), kind=kOutput, calls=%fused_computation.1 | convolution fusion | flops 8507473920 | bytes 27279360 | tf_op jit(solution)/shard_map/dot_general | solution.py:123
  249.6 133.7 %all_to_all.16 = bf16[4,8,40,2304]{3,2,1,0:T(8,128)(2,1)} all-to-all(bf16[4,8,40,2304]{3,2,1,0:T(8,128)(2,1)S(1)} %bitcast.61), channel_id=1, replica_groups=mesh['grp'=4,'ep'=8] {'grp'}, dimensions={0} | all-to-all | bytes 11796480 | tf_op jit(solution)/shard_map/all_to_all | solution.py:127
  383.3 5.1 %reduce_sum.75 = bf16[8,40,2304]{2,1,0:T(8,128)(2,1)} reduce(bf16[4,8,40,2304]{3,2,1,0:T(8,128)(2,1)} %all_to_all.16, bf16[]{:T(256)} %constant.59.clone.1), dimensions={0}, to_apply=%region_11.12 | reduce | flops 2211840 | bytes 7372802 | tf_op jit(solution)/shard_map/reduce_sum | solution.py:128
  388.4 3.8 all-to-all-start.2
  392.7 19.5 %all-to-all-done.2 = bf16[8,40,2304]{2,1,0:T(8,128)(2,1)S(1)} async-done(((bf16[8,40,2304]{2,1,0:T(8,128)(2,1)}), bf16[8,40,2304]{2,1,0:T(8,128)(2,1)S(1)}, u32[]{:S(2)}, u32[]{:S(2)}) %all-to-all-start.2) | async-done | bytes 1474592 | tf_op jit(solution)/shard_map/all_to_all | solution.py:129
  (58 shorter events, 10.0 us)
Async XLA Ops:
  6.5 385.7 %copy-start = (bf16[2304,8]{0,1:T(8,128)(2,1)S(1)}, bf16[2304,8]{0,1:T(8,128)(2,1)}, u32[]{:S(2)}) copy-start(bf16[2304,8]{0,1:T(8,128)(2,1)} %param.18) | copy-start | bytes 110596
  6.5 43.2 %copy-start.6 = (s32[1,128]{1,0:T(1,128)S(1)}, s32[1,128]{1,0:T(1,128)}, u32[]{:S(2)}) copy-start(s32[1,128]{1,0:T(1,128)} %param.15) | copy-start | bytes 1540
  6.5 204.6 %all-gather.3.cloned.1.call-start = ((), (), s32[]{:S(2)}) async-start(), calls=%async_computation.3 | async-start | bytes 7372800 | tf_op jit(solution)/shard_map/all_gather | solution.py:117
  6.5 19.1 %collective-permute-start.2 = (bf16[128,2304]{1,0:T(8,128)(2,1)}, bf16[128,2304]{1,0:T(8,128)(2,1)S(1)}, u32[]{:S(2)}, u32[]{:S(2)}) collective-permute-start(bf16[128,2304]{1,0:T(8,128)(2,1)} %bitcast.69), channel_id=1, source_target_pairs={{0,8},{8,16},{16,24},{1,9},{9,17},{17,25},{2,10},{10,18},{18,26},{... | collective-permute-start | bytes 1769480 | tf_op jit(solution)/shard_map/ppermute | solution.py:16
  11.6 19.1 %collective-permute-start = (s32[128]{0:T(128)}, s32[128]{0:T(128)S(1)}, u32[]{:S(2)}, u32[]{:S(2)}) collective-permute-start(s32[128]{0:T(128)} %bitcast.75), channel_id=1, source_target_pairs={{0,8},{8,16},{16,24},{1,9},{9,17},{17,25},{2,10},{10,18},{18,26},{... | collective-permute-start | bytes 1544 | tf_op jit(solution)/shard_map/ppermute | solution.py:16
  15.1 35.2 %collective-permute-start.4 = (bf16[128,2304]{1,0:T(8,128)(2,1)}, bf16[128,2304]{1,0:T(8,128)(2,1)S(1)}, u32[]{:S(2)}, u32[]{:S(2)}) collective-permute-start(bf16[128,2304]{1,0:T(8,128)(2,1)} %bitcast.70), channel_id=1, source_target_pairs={{0,8},{8,16},{16,24},{1,9},{9,17},{17,25},{2,10},{10,18},{18,26},{... | collective-permute-start | bytes 1769480 | tf_op jit(solution)/shard_map/ppermute | solution.py:16
  25.6 31.0 %collective-permute-start.3 = (bf16[128,2304]{1,0:T(8,128)(2,1)S(1)}, bf16[128,2304]{1,0:T(8,128)(2,1)}, u32[]{:S(2)}, u32[]{:S(2)}) collective-permute-start(bf16[128,2304]{1,0:T(8,128)(2,1)S(1)} %collective-permute-done.2), channel_id=1, source_target_pairs={{0,8},{8,16},{16,24},{1,9},{9,17},{17,25},{2,10},{10,18},{18,26},{... | collective-permute-start | bytes 1769480 | tf_op jit(solution)/shard_map/ppermute | solution.py:16
  30.7 19.0 %collective-permute-start.1 = (s32[128]{0:T(128)S(1)}, s32[128]{0:T(128)S(1)}, u32[]{:S(2)}, u32[]{:S(2)}) collective-permute-start(s32[128]{0:T(128)S(1)} %collective-permute-done), channel_id=1, source_target_pairs={{0,8},{8,16},{16,24},{1,9},{9,17},{17,25},{2,10},{10,18},{18,26},{... | collective-permute-start | bytes 1544 | tf_op jit(solution)/shard_map/ppermute | solution.py:16
  51.3 16.1 %collective-permute-start.5 = (bf16[128,2304]{1,0:T(8,128)(2,1)S(1)}, bf16[128,2304]{1,0:T(8,128)(2,1)}, u32[]{:S(2)}, u32[]{:S(2)}) collective-permute-start(bf16[128,2304]{1,0:T(8,128)(2,1)S(1)} %collective-permute-done.4), channel_id=1, source_target_pairs={{0,8},{8,16},{16,24},{1,9},{9,17},{17,25},{2,10},{10,18},{18,26},{... | collective-permute-start | bytes 1769480 | tf_op jit(solution)/shard_map/ppermute | solution.py:16
  59.1 9.7 %copy-start.1 = (bf16[1,128,2304]{1,2,0:T(8,128)(2,1)S(1)}, bf16[1,128,2304]{1,2,0:T(8,128)(2,1)}, u32[]{:S(2)}) copy-start(bf16[1,128,2304]{1,2,0:T(8,128)(2,1)} %copy.73) | copy-start | bytes 1769476
  59.2 9.7 %copy-start.2 = (bf16[128,2304]{0,1:T(8,128)(2,1)S(1)}, bf16[128,2304]{0,1:T(8,128)(2,1)}, u32[]{:S(2)}) copy-start(bf16[128,2304]{0,1:T(8,128)(2,1)} %copy.72) | copy-start | bytes 1769476
  68.9 2.9 copy-start.3
  71.8 5.8 %copy-start.4 = (f32[2304]{0:T(1024)S(1)}, f32[2304]{0:T(1024)}, u32[]{:S(2)}) copy-start(f32[2304]{0:T(1024)} %param.17) | copy-start | bytes 27652
  388.4 4.1 copy-start.5
  388.4 23.8 %all-to-all-start.2 = ((bf16[8,40,2304]{2,1,0:T(8,128)(2,1)}), bf16[8,40,2304]{2,1,0:T(8,128)(2,1)S(1)}, u32[]{:S(2)}, u32[]{:S(2)}) async-start(bf16[8,40,2304]{2,1,0:T(8,128)(2,1)} %reduce_sum.75), calls=%async_computation.2 | async-start | bytes 2949120 | tf_op jit(solution)/shard_map/all_to_all | solution.py:129
Sparse Core Ops, SparseCore 0:
  101.9 109.2 all-gather.2

commit v2 on v1

--- a/solution.py
+++ b/solution.py
@@ -124,8 +124,7 @@
         .astype(jnp.bfloat16)
         .reshape(n_grp, n_ep, capacity, width)
     )
-    slices = lax.all_to_all(partial_value, "grp", split_axis=0, concat_axis=0, tiled=True)
-    expert_output = jnp.sum(slices.astype(jnp.float32), axis=0).astype(jnp.bfloat16)
+    expert_output = lax.psum_scatter(partial_value, "grp", scatter_dimension=0, tiled=True)[0]
     summed = lax.all_to_all(expert_output, "ep", split_axis=0, concat_axis=0, tiled=True).reshape(
         n_slots, width
     )

time: 421 us -> 383 us (0.910)
  blocking collectives: 157 us -> 23.5 us
  waiting for transfers between devices: 148 us -> 250 us
  other arithmetic: 11.2 us -> 6.14 us
    all_to_all x1 -> x0, blocking collectives: 134 us -> none  [local(): lax.all_to_all(partial_value, 'grp', split_axis=0, concat_axis=0, tiled=T...]
    reduce_scatter x0 -> x1, waiting for transfers between devices: none -> 103 us  [local(): lax.psum_scatter(partial_value, 'grp', scatter_dimension=0, tiled=True)[0]]
    reduce_sum x1 -> x0, other arithmetic: 5.1 us -> none  [local(): jnp.sum(slices.astype(jnp.float32), axis=0).astype(jnp.bfloat16)]
  transfers between devices with their start and end apart: 8 -> 9, of which waited for: 5 -> 6; matrix products, arithmetic and copies ran while one was open for 4% -> 4% of each run, Pallas kernels for 0% -> 0%
where the time goes in v2:
time: 383 us; the launch traced here: 382 us
  waiting for transfers between devices  250 us (65%)
  matrix products  48.3 us (13%)
  starting transfers between devices  29 us (8%)
  blocking collectives  23.5 us (6%)
  between operations  13.7 us (4%)
  local copies, waits for them, and re-layouts  10.9 us (3%)
  other arithmetic  6.14 us (2%)
    all_gather x1, waiting for transfers between devices, local(): lax.all_gather(in_plane, 'grp', axis=0, tiled=False)  109 us
    reduce_scatter x1, waiting for transfers between devices, local(): lax.psum_scatter(partial_value, 'grp', scatter_dimension=0, tiled=True)[0]  103 us
    ppermute x6, starting transfers between devices, shift_up(): return lax.ppermute(x, 'grp', perm=[(i, i + 1) for i in range(n_grp - 1)])  25.1 us
    all_to_all x1, blocking collectives, local(): lax.all_to_all(outgoing, 'ep', split_axis=0, concat_axis=0, tiled=True)  23.5 us
    dot_general x1, matrix products, local(): both = jnp.dot(arrived, weight_matrix, preferred_element_type=jnp.float32)  21.8 us
    all_to_all x1, waiting for transfers between devices, local(): lax.all_to_all(expert_output, 'ep', split_axis=0, concat_axis=0, tiled=True)  19.5 us
    ppermute x6, waiting for transfers between devices, shift_up(): return lax.ppermute(x, 'grp', perm=[(i, i + 1) for i in range(n_grp - 1)])  19 us
    dot_general x1, matrix products, local(): jnp.dot(hidden, weight_out, preferred_element_type=jnp.float32)  14.5 us
  transfers between devices with their start and end apart: 9, of which 6 were waited for; matrix products, arithmetic and copies ran while one was open for 4% of the time, Pallas kernels for 0%

profile of v2, /device:TPU:0, one launch (start us, length us, event | category | flops | bytes accessed | tf_op | source)
XLA Modules:
  0.0 382.1 jit_solution(3346502823672597476)
XLA Ops:
  6.5 5.1 %collective-permute-start.2 = (bf16[128,2304]{1,0:T(8,128)(2,1)}, bf16[128,2304]{1,0:T(8,128)(2,1)S(1)}, u32[]{:S(2)}, u32[]{:S(2)}) collective-permute-start(bf16[128,2304]{1,0:T(8,128)(2,1)} %bitcast.71), channel_id=1, source_target_pairs={{0,8},{8,16},{16,24},{1,9},{9,17},{17,25},{2,10},{10,18},{18,26},{... | collective-permute-start | bytes 1769480 | tf_op jit(solution)/shard_map/ppermute | solution.py:16
  11.6 3.4 collective-permute-start
  15.1 3.5 collective-permute-start.4
  22.1 3.5 collective-permute-done.2
  25.6 5.1 %collective-permute-start.3 = (bf16[128,2304]{1,0:T(8,128)(2,1)S(1)}, bf16[128,2304]{1,0:T(8,128)(2,1)}, u32[]{:S(2)}, u32[]{:S(2)}) collective-permute-start(bf16[128,2304]{1,0:T(8,128)(2,1)S(1)} %collective-permute-done.2), channel_id=1, source_target_pairs={{0,8},{8,16},{16,24},{1,9},{9,17},{17,25},{2,10},{10,18},{18,26},{... | collective-permute-start | bytes 1769480 | tf_op jit(solution)/shard_map/ppermute | solution.py:16
  30.7 2.7 collective-permute-start.1
  33.5 1.4 copy.69
  34.8 2.1 copy.73
  36.9 1.4 copy.70
  38.3 11.4 %collective-permute-done.1 = s32[128]{0:T(128)S(1)} collective-permute-done((s32[128]{0:T(128)S(1)}, s32[128]{0:T(128)S(1)}, u32[]{:S(2)}, u32[]{:S(2)}) %collective-permute-start.1) | collective-permute-done | bytes 544 | tf_op jit(solution)/shard_map/ppermute | solution.py:16
  51.3 5.3 %collective-permute-start.5 = (bf16[128,2304]{1,0:T(8,128)(2,1)S(1)}, bf16[128,2304]{1,0:T(8,128)(2,1)}, u32[]{:S(2)}, u32[]{:S(2)}) collective-permute-start(bf16[128,2304]{1,0:T(8,128)(2,1)S(1)} %collective-permute-done.4), channel_id=1, source_target_pairs={{0,8},{8,16},{16,24},{1,9},{9,17},{17,25},{2,10},{10,18},{18,26},{... | collective-permute-start | bytes 1769480 | tf_op jit(solution)/shard_map/ppermute | solution.py:16
  56.6 1.4 copy.67
  59.2 4.2 %fusion.46 = (f32[36,128]{1,0:T(8,128)S(1)}, bf16[36,128,384]{1,2,0:T(8,128)(2,1)}) fusion(f32[36,384,128]{2,1,0:T(8,128)S(1)} %fusion.18, pred[128,384]{0,1:T(8,128)(4,1)S(1)} %compare_and_fusion), kind=kOutput, calls=%fused_computation.69 | output fusion | flops 14156159 | bytes 10684416 | tf_op jit(solution)/shard_map/sub | solution.py:69
  63.4 4.1 %collective-permute-done.5 = bf16[128,2304]{1,0:T(8,128)(2,1)} collective-permute-done((bf16[128,2304]{1,0:T(8,128)(2,1)S(1)}, bf16[128,2304]{1,0:T(8,128)(2,1)}, u32[]{:S(2)}, u32[]{:S(2)}) %collective-permute-start.5) | collective-permute-done | bytes 589856 | tf_op jit(solution)/shard_map/ppermute | solution.py:16
  67.5 1.4 copy.71
  68.9 2.9 divide_convert_fusion
  71.8 5.7 %multiply_reduce_fusion = (f32[128]{0:T(128)S(1)}, f32[128,2304]{1,0:T(8,128)S(1)}) fusion(bf16[128,2304]{0,1:T(8,128)(2,1)S(1)} %bitcast.70, bf16[2304,2304]{1,0:T(8,128)(2,1)} %param.16, bf16[1,128,2304]{2,1,0:T(8,128)(2,1)S(1)} %copy-done.3), kind=kOutput, calls=%fused_computation.32 | convolution fusion | flops 1360134016 | bytes 12976640 | tf_op jit(solution)/shard_map/dot_general | solution.py:79
  78.2 23.5 %all_to_all.10 = bf16[8,40,2304]{2,1,0:T(8,128)(2,1)} all-to-all(bf16[8,40,2304]{2,1,0:T(8,128)(2,1)S(1)} %bitcast.64), channel_id=1, replica_groups=mesh['grp'=4,'ep'=8] {'ep'}, dimensions={0} | all-to-all | bytes 2949120 | tf_op jit(solution)/shard_map/all_to_all | solution.py:116
  102.0 109.2 %all-gather.3.cloned.1.call-done = bf16[32,40,2304]{2,1,0:T(8,128)(2,1)} async-done(((bf16[8,40,2304]{2,1,0:T(8,128)(2,1)}), bf16[32,40,2304]{2,1,0:T(8,128)(2,1)}) %all-gather.3.cloned.1.call-update) | async-done | bytes 5898256 | tf_op jit(solution)/shard_map/all_gather | solution.py:117
  211.2 21.8 %fusion.47 = f32[1280,2880]{0,1:T(8,128)S(1)} fusion(bf16[1280,2304]{1,0:T(8,128)(2,1)} %bitcast.81, bf16[2304,2880]{0,1:T(8,128)(2,1)} %bitcast.80), kind=kOutput, calls=%fused_computation.70 | convolution fusion | flops 16986931200 | bytes 33914880 | tf_op jit(solution)/shard_map/dot_general | solution.py:120
  232.9 14.5 %convolution_convert_fusion = bf16[1280,2304]{1,0:T(8,128)(2,1)} fusion(bf16[1,1440,2304]{2,1,0:T(8,128)(2,1)} %param.21, f32[1280,2880]{0,1:T(8,128)S(1)} %fusion.47), kind=kOutput, calls=%fused_computation.1 | convolution fusion | flops 8507473920 | bytes 27279360 | tf_op jit(solution)/shard_map/dot_general | solution.py:123
  247.5 102.8 %reduce-scatter.2.cloned.1.call-done = bf16[1,8,40,2304]{3,2,1,0:T(8,128)(2,1)} async-done(((bf16[4,8,40,2304]{3,2,1,0:T(8,128)(2,1)}), bf16[1,8,40,2304]{3,2,1,0:T(8,128)(2,1)}) %reduce-scatter.2.cloned.1.call-update) | async-done | bytes 1474576 | tf_op jit(solution)/shard_map/reduce_scatter | solution.py:127
  350.3 3.7 all-to-all-start.1
  354.4 19.5 %all-to-all-done.1 = bf16[8,40,2304]{2,1,0:T(8,128)(2,1)S(1)} async-done(((bf16[8,40,2304]{2,1,0:T(8,128)(2,1)}), bf16[8,40,2304]{2,1,0:T(8,128)(2,1)S(1)}, u32[]{:S(2)}, u32[]{:S(2)}) %all-to-all-start.1) | async-done | bytes 1474592 | tf_op jit(solution)/shard_map/all_to_all | solution.py:128
  (59 shorter events, 8.9 us)
Async XLA Ops:
  6.5 347.4 %copy-start = (bf16[2304,8]{0,1:T(8,128)(2,1)S(1)}, bf16[2304,8]{0,1:T(8,128)(2,1)}, u32[]{:S(2)}) copy-start(bf16[2304,8]{0,1:T(8,128)(2,1)} %param.18) | copy-start | bytes 110596
  6.5 43.2 %copy-start.6 = (s32[1,128]{1,0:T(1,128)S(1)}, s32[1,128]{1,0:T(1,128)}, u32[]{:S(2)}) copy-start(s32[1,128]{1,0:T(1,128)} %param.15) | copy-start | bytes 1540
  6.5 204.6 %all-gather.3.cloned.1.call-start = ((), (), s32[]{:S(2)}) async-start(), calls=%async_computation.4 | async-start | bytes 7372800 | tf_op jit(solution)/shard_map/all_gather | solution.py:117
  6.5 19.1 %collective-permute-start.2 = (bf16[128,2304]{1,0:T(8,128)(2,1)}, bf16[128,2304]{1,0:T(8,128)(2,1)S(1)}, u32[]{:S(2)}, u32[]{:S(2)}) collective-permute-start(bf16[128,2304]{1,0:T(8,128)(2,1)} %bitcast.71), channel_id=1, source_target_pairs={{0,8},{8,16},{16,24},{1,9},{9,17},{17,25},{2,10},{10,18},{18,26},{... | collective-permute-start | bytes 1769480 | tf_op jit(solution)/shard_map/ppermute | solution.py:16
  11.6 19.1 %collective-permute-start = (s32[128]{0:T(128)}, s32[128]{0:T(128)S(1)}, u32[]{:S(2)}, u32[]{:S(2)}) collective-permute-start(s32[128]{0:T(128)} %bitcast.77), channel_id=1, source_target_pairs={{0,8},{8,16},{16,24},{1,9},{9,17},{17,25},{2,10},{10,18},{18,26},{... | collective-permute-start | bytes 1544 | tf_op jit(solution)/shard_map/ppermute | solution.py:16
  15.1 35.2 %collective-permute-start.4 = (bf16[128,2304]{1,0:T(8,128)(2,1)}, bf16[128,2304]{1,0:T(8,128)(2,1)S(1)}, u32[]{:S(2)}, u32[]{:S(2)}) collective-permute-start(bf16[128,2304]{1,0:T(8,128)(2,1)} %bitcast.72), channel_id=1, source_target_pairs={{0,8},{8,16},{16,24},{1,9},{9,17},{17,25},{2,10},{10,18},{18,26},{... | collective-permute-start | bytes 1769480 | tf_op jit(solution)/shard_map/ppermute | solution.py:16
  25.6 31.0 %collective-permute-start.3 = (bf16[128,2304]{1,0:T(8,128)(2,1)S(1)}, bf16[128,2304]{1,0:T(8,128)(2,1)}, u32[]{:S(2)}, u32[]{:S(2)}) collective-permute-start(bf16[128,2304]{1,0:T(8,128)(2,1)S(1)} %collective-permute-done.2), channel_id=1, source_target_pairs={{0,8},{8,16},{16,24},{1,9},{9,17},{17,25},{2,10},{10,18},{18,26},{... | collective-permute-start | bytes 1769480 | tf_op jit(solution)/shard_map/ppermute | solution.py:16
  30.7 19.0 %collective-permute-start.1 = (s32[128]{0:T(128)S(1)}, s32[128]{0:T(128)S(1)}, u32[]{:S(2)}, u32[]{:S(2)}) collective-permute-start(s32[128]{0:T(128)S(1)} %collective-permute-done), channel_id=1, source_target_pairs={{0,8},{8,16},{16,24},{1,9},{9,17},{17,25},{2,10},{10,18},{18,26},{... | collective-permute-start | bytes 1544 | tf_op jit(solution)/shard_map/ppermute | solution.py:16
  51.3 16.1 %collective-permute-start.5 = (bf16[128,2304]{1,0:T(8,128)(2,1)S(1)}, bf16[128,2304]{1,0:T(8,128)(2,1)}, u32[]{:S(2)}, u32[]{:S(2)}) collective-permute-start(bf16[128,2304]{1,0:T(8,128)(2,1)S(1)} %collective-permute-done.4), channel_id=1, source_target_pairs={{0,8},{8,16},{16,24},{1,9},{9,17},{17,25},{2,10},{10,18},{18,26},{... | collective-permute-start | bytes 1769480 | tf_op jit(solution)/shard_map/ppermute | solution.py:16
  59.1 9.7 %copy-start.1 = (bf16[1,128,2304]{1,2,0:T(8,128)(2,1)S(1)}, bf16[1,128,2304]{1,2,0:T(8,128)(2,1)}, u32[]{:S(2)}) copy-start(bf16[1,128,2304]{1,2,0:T(8,128)(2,1)} %copy.73) | copy-start | bytes 1769476
  59.2 9.7 %copy-start.2 = (bf16[128,2304]{0,1:T(8,128)(2,1)S(1)}, bf16[128,2304]{0,1:T(8,128)(2,1)}, u32[]{:S(2)}) copy-start(bf16[128,2304]{0,1:T(8,128)(2,1)} %copy.72) | copy-start | bytes 1769476
  68.9 2.9 copy-start.3
  71.8 5.8 %copy-start.4 = (f32[2304]{0:T(1024)S(1)}, f32[2304]{0:T(1024)}, u32[]{:S(2)}) copy-start(f32[2304]{0:T(1024)} %param.17) | copy-start | bytes 27652
  101.8 248.5 %reduce-scatter.2.cloned.1.call-start = ((), (), s32[]{:S(2)}) async-start(), calls=%async_computation.3 | async-start | bytes 7372800 | tf_op jit(solution)/shard_map/reduce_scatter | solution.py:127
  247.5 106.8 %copy-start.5 = (s32[1,128,2]{1,2,0:T(2,128)S(1)}, s32[1,128,2]{1,2,0:T(2,128)}, u32[]{:S(2)}) copy-start(s32[1,128,2]{1,2,0:T(2,128)} %param.19) | copy-start | bytes 3076
  350.3 23.6 %all-to-all-start.1 = ((bf16[8,40,2304]{2,1,0:T(8,128)(2,1)}), bf16[8,40,2304]{2,1,0:T(8,128)(2,1)S(1)}, u32[]{:S(2)}, u32[]{:S(2)}) async-start(bf16[8,40,2304]{2,1,0:T(8,128)(2,1)} %bitcast.69), calls=%async_computation.2 | async-start | bytes 2949120 | tf_op jit(solution)/shard_map/all_to_all | solution.py:128
Sparse Core Ops, SparseCore 0:
  101.9 109.2 all-gather.2
  247.6 102.6 reduce-scatter.1

commit v3 on v2

--- a/solution.py
+++ b/solution.py
@@ -113,21 +113,25 @@
     weight_out = expert_out[0]
     ff_here = weight_in.shape[2]
     weight_matrix = weight_in.reshape(width, 2 * ff_here)
-    in_plane = lax.all_to_all(outgoing, "ep", split_axis=0, concat_axis=0, tiled=True)
-    arrived = lax.all_gather(in_plane, "grp", axis=0, tiled=False).reshape(
-        n_grp * n_slots, width
-    )
-    both = jnp.dot(arrived, weight_matrix, preferred_element_type=jnp.float32)
-    hidden = (jax.nn.silu(both[:, :ff_here]) * both[:, ff_here:]).astype(jnp.bfloat16)
-    partial_value = (
-        jnp.dot(hidden, weight_out, preferred_element_type=jnp.float32)
-        .astype(jnp.bfloat16)
-        .reshape(n_grp, n_ep, capacity, width)
-    )
-    expert_output = lax.psum_scatter(partial_value, "grp", scatter_dimension=0, tiled=True)[0]
-    summed = lax.all_to_all(expert_output, "ep", split_axis=0, concat_axis=0, tiled=True).reshape(
-        n_slots, width
-    )
+    n_chunks = 2 if capacity % 2 == 0 else 1
+    per_chunk = capacity // n_chunks
+    returned = []
+    for c in range(n_chunks):
+        piece = outgoing[:, c * per_chunk : (c + 1) * per_chunk]
+        in_plane = lax.all_to_all(piece, "ep", split_axis=0, concat_axis=0, tiled=True)
+        arrived = lax.all_gather(in_plane, "grp", axis=0, tiled=False).reshape(-1, width)
+        both = jnp.dot(arrived, weight_matrix, preferred_element_type=jnp.float32)
+        hidden = (jax.nn.silu(both[:, :ff_here]) * both[:, ff_here:]).astype(jnp.bfloat16)
+        partial_value = (
+            jnp.dot(hidden, weight_out, preferred_element_type=jnp.float32)
+            .astype(jnp.bfloat16)
+            .reshape(n_grp, n_ep, per_chunk, width)
+        )
+        expert_output = lax.psum_scatter(partial_value, "grp", scatter_dimension=0, tiled=True)[0]
+        returned.append(
+            lax.all_to_all(expert_output, "ep", split_axis=0, concat_axis=0, tiled=True)
+        )
+    summed = jnp.concatenate(returned, axis=1).reshape(n_slots, width)
     moe = jnp.dot(combine, summed, preferred_element_type=jnp.float32)
     return (residual + moe).astype(jnp.bfloat16)[None]
 

time: 383 us -> 381 us (level)
  waiting for transfers between devices: 250 us -> 189 us
  local copies, waits for them, and re-layouts: 10.9 us -> 45.2 us
  matrix products: 48.3 us -> 59.5 us
  blocking collectives: 23.5 us -> 33.1 us
  starting transfers between devices: 29 us -> 32.9 us
    all_gather x1 -> x2, waiting for transfers between devices: 109 us -> 63.9 us  [local(): lax.all_gather(in_plane, 'grp', axis=0, tiled=False).reshape(-1, width)]
    reshape x0 -> x4, local copies, waits for them, and re-layouts: none -> 21.6 us  [the longest x2 10.9 us: local(): lax.all_gather(in_plane, 'grp', axis=0, tiled=False).reshape(-1, width)]
    all_gather x0 -> x2, local copies, waits for them, and re-layouts: none -> 10.5 us  [local(): lax.all_gather(in_plane, 'grp', axis=0, tiled=False).reshape(-1, width)]
    reduce_scatter x1 -> x2, waiting for transfers between devices: 103 us -> 92.7 us  [local(): lax.psum_scatter(partial_value, 'grp', scatter_dimension=0, tiled=True)[0]]
    all_to_all x1 -> x2, blocking collectives: 23.5 us -> 33.1 us  [local(): lax.all_to_all(piece, 'ep', split_axis=0, concat_axis=0, tiled=True)]
    dot_general x1 -> x2, matrix products: 21.8 us -> 28.2 us  [local(): both = jnp.dot(arrived, weight_matrix, preferred_element_type=jnp.float32)]
    all_to_all x1 -> x2, waiting for transfers between devices: 19.5 us -> 13.2 us  [local(): lax.all_to_all(expert_output, 'ep', split_axis=0, concat_axis=0, tiled=True)]
    dot_general x1 -> x2, matrix products: 14.5 us -> 19.3 us  [local(): jnp.dot(hidden, weight_out, preferred_element_type=jnp.float32)]
  transfers between devices with their start and end apart: 9 -> 12, of which waited for: 6 -> 8; matrix products, arithmetic and copies ran while one was open for 4% -> 26% of each run, Pallas kernels for 0% -> 0%
where the time goes in v3:
time: 381 us; the launch traced here: 380 us
  waiting for transfers between devices  189 us (50%)
  matrix products  59.5 us (16%)
  local copies, waits for them, and re-layouts  45.2 us (12%)
  blocking collectives  33.1 us (9%)
  starting transfers between devices  32.9 us (9%)
  between operations  13.4 us (4%)
  other arithmetic  6.3 us (2%)
    reduce_scatter x2, waiting for transfers between devices, local(): lax.psum_scatter(partial_value, 'grp', scatter_dimension=0, tiled=True)[0]  92.7 us
    all_gather x2, waiting for transfers between devices, local(): lax.all_gather(in_plane, 'grp', axis=0, tiled=False).reshape(-1, width)  63.9 us
    all_to_all x2, blocking collectives, local(): lax.all_to_all(piece, 'ep', split_axis=0, concat_axis=0, tiled=True)  33.1 us
    dot_general x2, matrix products, local(): both = jnp.dot(arrived, weight_matrix, preferred_element_type=jnp.float32)  28.2 us
    ppermute x6, starting transfers between devices, shift_up(): return lax.ppermute(x, 'grp', perm=[(i, i + 1) for i in range(n_grp - 1)])  25.1 us
    dot_general x2, matrix products, local(): jnp.dot(hidden, weight_out, preferred_element_type=jnp.float32)  19.3 us
    ppermute x6, waiting for transfers between devices, shift_up(): return lax.ppermute(x, 'grp', perm=[(i, i + 1) for i in range(n_grp - 1)])  19.2 us
    all_to_all x2, waiting for transfers between devices, local(): lax.all_to_all(expert_output, 'ep', split_axis=0, concat_axis=0, tiled=True)  13.2 us
  transfers between devices with their start and end apart: 12, of which 8 were waited for; matrix products, arithmetic and copies ran while one was open for 26% of the time, Pallas kernels for 0%

profile of v3, /device:TPU:0, one launch (start us, length us, event | category | flops | bytes accessed | tf_op | source)
XLA Modules:
  0.0 379.6 jit_solution(13655963767902462419)
XLA Ops:
  6.5 5.1 %collective-permute-start.2 = (bf16[128,2304]{1,0:T(8,128)(2,1)}, bf16[128,2304]{1,0:T(8,128)(2,1)S(1)}, u32[]{:S(2)}, u32[]{:S(2)}) collective-permute-start(bf16[128,2304]{1,0:T(8,128)(2,1)} %bitcast.78), channel_id=1, source_target_pairs={{0,8},{8,16},{16,24},{1,9},{9,17},{17,25},{2,10},{10,18},{18,26},{... | collective-permute-start | bytes 1769480 | tf_op jit(solution)/shard_map/ppermute | solution.py:16
  25.6 5.1 %collective-permute-start.3 = (bf16[128,2304]{1,0:T(8,128)(2,1)S(1)}, bf16[128,2304]{1,0:T(8,128)(2,1)}, u32[]{:S(2)}, u32[]{:S(2)}) collective-permute-start(bf16[128,2304]{1,0:T(8,128)(2,1)S(1)} %collective-permute-done.2), channel_id=1, source_target_pairs={{0,8},{8,16},{16,24},{1,9},{9,17},{17,25},{2,10},{10,18},{18,26},{... | collective-permute-start | bytes 1769480 | tf_op jit(solution)/shard_map/ppermute | solution.py:16
  38.3 11.4 %collective-permute-done.1 = s32[128]{0:T(128)S(1)} collective-permute-done((s32[128]{0:T(128)S(1)}, s32[128]{0:T(128)S(1)}, u32[]{:S(2)}, u32[]{:S(2)}) %collective-permute-start.1) | collective-permute-done | bytes 544 | tf_op jit(solution)/shard_map/ppermute | solution.py:16
  51.3 5.3 %collective-permute-start.5 = (bf16[128,2304]{1,0:T(8,128)(2,1)S(1)}, bf16[128,2304]{1,0:T(8,128)(2,1)}, u32[]{:S(2)}, u32[]{:S(2)}) collective-permute-start(bf16[128,2304]{1,0:T(8,128)(2,1)S(1)} %collective-permute-done.4), channel_id=1, source_target_pairs={{0,8},{8,16},{16,24},{1,9},{9,17},{17,25},{2,10},{10,18},{18,26},{... | collective-permute-start | bytes 1769480 | tf_op jit(solution)/shard_map/ppermute | solution.py:16
  59.1 4.1 %fusion.60 = (f32[36,128]{1,0:T(8,128)S(1)}, bf16[36,128,384]{1,2,0:T(8,128)(2,1)}) fusion(f32[36,384,128]{2,1,0:T(8,128)S(1)} %fusion.30, pred[128,384]{0,1:T(8,128)(4,1)S(1)} %compare_and_fusion), kind=kOutput, calls=%fused_computation.79 | output fusion | flops 14156159 | bytes 10684416 | tf_op jit(solution)/shard_map/sub | solution.py:69
  63.2 4.2 %collective-permute-done.5 = bf16[128,2304]{1,0:T(8,128)(2,1)} collective-permute-done((bf16[128,2304]{1,0:T(8,128)(2,1)S(1)}, bf16[128,2304]{1,0:T(8,128)(2,1)}, u32[]{:S(2)}, u32[]{:S(2)}) %collective-permute-start.5) | collective-permute-done | bytes 589856 | tf_op jit(solution)/shard_map/ppermute | solution.py:16
  71.8 5.7 %multiply_reduce_fusion = (f32[128]{0:T(128)S(1)}, f32[128,2304]{1,0:T(8,128)S(1)}) fusion(bf16[128,2304]{0,1:T(8,128)(2,1)S(1)} %bitcast.75, bf16[2304,2304]{1,0:T(8,128)(2,1)} %param.16, bf16[1,128,2304]{2,1,0:T(8,128)(2,1)S(1)} %copy-done.3), kind=kOutput, calls=%fused_computation.40 | convolution fusion | flops 1360134016 | bytes 12976640 | tf_op jit(solution)/shard_map/dot_general | solution.py:79
  78.4 17.1 %all_to_all.20 = bf16[8,20,2304]{2,1,0:T(8,128)(2,1)S(1)} all-to-all(bf16[8,20,2304]{2,1,0:T(8,128)(2,1)S(1)} %get-tuple-element.6), channel_id=1, replica_groups=mesh['grp'=4,'ep'=8] {'ep'}, dimensions={0} | all-to-all | bytes 1474560 | tf_op jit(solution)/shard_map/all_to_all | solution.py:121
  96.6 16.0 %all_to_all.21 = bf16[8,20,2304]{2,1,0:T(8,128)(2,1)S(1)} all-to-all(bf16[8,20,2304]{2,1,0:T(8,128)(2,1)S(1)} %get-tuple-element.5), channel_id=1, replica_groups=mesh['grp'=4,'ep'=8] {'ep'}, dimensions={0} | all-to-all | bytes 1474560 | tf_op jit(solution)/shard_map/all_to_all | solution.py:121
  113.9 43.4 %all-gather.7.cloned.1.call-done = bf16[32,20,2304]{2,0,1:T(8,128)(2,1)} async-done(((bf16[8,20,2304]{2,0,1:T(8,128)(2,1)}), bf16[32,20,2304]{2,0,1:T(8,128)(2,1)}) %all-gather.7.cloned.1.call-update) | async-done | bytes 2949136 | tf_op jit(solution)/shard_map/all_gather | solution.py:122
  157.3 5.2 %copy.108 = bf16[32,20,2304]{2,1,0:T(8,128)(2,1)} copy(bf16[32,20,2304]{2,0,1:T(8,128)(2,1)} %all-gather.7.cloned.1.call-done) | data formatting | bytes 5898240 | tf_op jit(solution)/shard_map/all_gather | solution.py:122
  162.5 5.4 %reshape.218 = bf16[640,2304]{1,0:T(8,128)(2,1)} reshape(bf16[32,20,2304]{2,1,0:T(8,128)(2,1)} %copy.108) | data formatting | bytes 5898240 | tf_op jit(solution)/shard_map/reshape | solution.py:122
  168.0 14.1 %fusion.62 = f32[640,2880]{0,1:T(8,128)S(1)} fusion(bf16[640,2304]{1,0:T(8,128)(2,1)} %reshape.218, bf16[2304,2880]{0,1:T(8,128)(2,1)} %bitcast.87), kind=kOutput, calls=%fused_computation.81 | convolution fusion | flops 8493465600 | bytes 23592960 | tf_op jit(solution)/shard_map/dot_general | solution.py:123
  182.1 9.7 %fusion.9 = bf16[640,2304]{1,0:T(8,128)(2,1)} fusion(bf16[1,1440,2304]{2,1,0:T(8,128)(2,1)} %param.21, f32[640,2880]{0,1:T(8,128)S(1)} %fusion.62), kind=kOutput, calls=%fused_computation.9 | convolution fusion | flops 4253736960 | bytes 16957440 | tf_op jit(solution)/shard_map/dot_general | solution.py:126
  191.7 5.3 %reshape.219 = bf16[4,8,20,2304]{3,2,1,0:T(8,128)(2,1)} reshape(bf16[640,2304]{1,0:T(8,128)(2,1)} %fusion.9) | data formatting | bytes 5898240 | tf_op jit(solution)/shard_map/reshape | solution.py:128
  197.3 20.5 %all-gather.5.cloned.1.call-done = bf16[32,20,2304]{2,0,1:T(8,128)(2,1)} async-done(((bf16[8,20,2304]{2,0,1:T(8,128)(2,1)}), bf16[32,20,2304]{2,0,1:T(8,128)(2,1)}) %all-gather.5.cloned.1.call-update) | async-done | bytes 2949136 | tf_op jit(solution)/shard_map/all_gather | solution.py:122
  217.8 5.3 %copy.106 = bf16[32,20,2304]{2,1,0:T(8,128)(2,1)} copy(bf16[32,20,2304]{2,0,1:T(8,128)(2,1)} %all-gather.5.cloned.1.call-done) | data formatting | bytes 5898240 | tf_op jit(solution)/shard_map/all_gather | solution.py:122
  223.1 5.5 %reshape.216 = bf16[640,2304]{1,0:T(8,128)(2,1)} reshape(bf16[32,20,2304]{2,1,0:T(8,128)(2,1)} %copy.106) | data formatting | bytes 5898240 | tf_op jit(solution)/shard_map/reshape | solution.py:122
  228.6 14.1 %fusion.61 = f32[640,2880]{0,1:T(8,128)S(1)} fusion(bf16[640,2304]{1,0:T(8,128)(2,1)} %reshape.216, bf16[2304,2880]{0,1:T(8,128)(2,1)} %bitcast.88), kind=kOutput, calls=%fused_computation.80 | convolution fusion | flops 8493465600 | bytes 23592960 | tf_op jit(solution)/shard_map/dot_general | solution.py:123
  242.7 9.7 %fusion.6 = bf16[640,2304]{1,0:T(8,128)(2,1)} fusion(bf16[1,1440,2304]{2,1,0:T(8,128)(2,1)} %param.21, f32[640,2880]{0,1:T(8,128)S(1)} %fusion.61), kind=kOutput, calls=%fused_computation.8 | convolution fusion | flops 4253736960 | bytes 16957440 | tf_op jit(solution)/shard_map/dot_general | solution.py:126
  252.4 5.4 %reshape.217 = bf16[4,8,20,2304]{3,2,1,0:T(8,128)(2,1)} reshape(bf16[640,2304]{1,0:T(8,128)(2,1)} %fusion.6) | data formatting | bytes 5898240 | tf_op jit(solution)/shard_map/reshape | solution.py:128
  257.8 27.5 %reduce-scatter.5.cloned.1.call-done = bf16[1,8,20,2304]{3,2,1,0:T(8,128)(2,1)} async-done(((bf16[4,8,20,2304]{3,2,1,0:T(8,128)(2,1)}), bf16[1,8,20,2304]{3,2,1,0:T(8,128)(2,1)}) %reduce-scatter.5.cloned.1.call-update) | async-done | bytes 737296 | tf_op jit(solution)/shard_map/reduce_scatter | solution.py:130
  288.9 65.2 %reduce-scatter.3.cloned.1.call-done = bf16[1,8,20,2304]{3,2,1,0:T(8,128)(2,1)} async-done(((bf16[4,8,20,2304]{3,2,1,0:T(8,128)(2,1)}), bf16[1,8,20,2304]{3,2,1,0:T(8,128)(2,1)}) %reduce-scatter.3.cloned.1.call-update) | async-done | bytes 737296 | tf_op jit(solution)/shard_map/reduce_scatter | solution.py:130
  358.3 13.2 %all-to-all-done.1 = bf16[8,20,2304]{2,1,0:T(8,128)(2,1)S(1)} async-done(((bf16[8,20,2304]{2,1,0:T(8,128)(2,1)}), bf16[8,20,2304]{2,1,0:T(8,128)(2,1)S(1)}, u32[]{:S(2)}, u32[]{:S(2)}) %all-to-all-start.1) | async-done | bytes 737312 | tf_op jit(solution)/shard_map/all_to_all | solution.py:132
  (80 shorter events, 42.7 us)
Async XLA Ops:
  6.5 351.2 %copy-start = (bf16[2304,8]{0,1:T(8,128)(2,1)S(1)}, bf16[2304,8]{0,1:T(8,128)(2,1)}, u32[]{:S(2)}) copy-start(bf16[2304,8]{0,1:T(8,128)(2,1)} %param.18) | copy-start | bytes 110596
  6.5 43.2 %copy-start.6 = (s32[1,128]{1,0:T(1,128)S(1)}, s32[1,128]{1,0:T(1,128)}, u32[]{:S(2)}) copy-start(s32[1,128]{1,0:T(1,128)} %param.15) | copy-start | bytes 1540
  6.5 150.8 %all-gather.7.cloned.1.call-start = ((), (), s32[]{:S(2)}) async-start(), calls=%async_computation.9 | async-start | bytes 3686400 | tf_op jit(solution)/shard_map/all_gather | solution.py:122
  6.5 19.1 %collective-permute-start.2 = (bf16[128,2304]{1,0:T(8,128)(2,1)}, bf16[128,2304]{1,0:T(8,128)(2,1)S(1)}, u32[]{:S(2)}, u32[]{:S(2)}) collective-permute-start(bf16[128,2304]{1,0:T(8,128)(2,1)} %bitcast.78), channel_id=1, source_target_pairs={{0,8},{8,16},{16,24},{1,9},{9,17},{17,25},{2,10},{10,18},{18,26},{... | collective-permute-start | bytes 1769480 | tf_op jit(solution)/shard_map/ppermute | solution.py:16
  11.6 19.1 %collective-permute-start = (s32[128]{0:T(128)}, s32[128]{0:T(128)S(1)}, u32[]{:S(2)}, u32[]{:S(2)}) collective-permute-start(s32[128]{0:T(128)} %bitcast.84), channel_id=1, source_target_pairs={{0,8},{8,16},{16,24},{1,9},{9,17},{17,25},{2,10},{10,18},{18,26},{... | collective-permute-start | bytes 1544 | tf_op jit(solution)/shard_map/ppermute | solution.py:16
  15.1 35.2 %collective-permute-start.4 = (bf16[128,2304]{1,0:T(8,128)(2,1)}, bf16[128,2304]{1,0:T(8,128)(2,1)S(1)}, u32[]{:S(2)}, u32[]{:S(2)}) collective-permute-start(bf16[128,2304]{1,0:T(8,128)(2,1)} %bitcast.79), channel_id=1, source_target_pairs={{0,8},{8,16},{16,24},{1,9},{9,17},{17,25},{2,10},{10,18},{18,26},{... | collective-permute-start | bytes 1769480 | tf_op jit(solution)/shard_map/ppermute | solution.py:16
  25.6 31.0 %collective-permute-start.3 = (bf16[128,2304]{1,0:T(8,128)(2,1)S(1)}, bf16[128,2304]{1,0:T(8,128)(2,1)}, u32[]{:S(2)}, u32[]{:S(2)}) collective-permute-start(bf16[128,2304]{1,0:T(8,128)(2,1)S(1)} %collective-permute-done.2), channel_id=1, source_target_pairs={{0,8},{8,16},{16,24},{1,9},{9,17},{17,25},{2,10},{10,18},{18,26},{... | collective-permute-start | bytes 1769480 | tf_op jit(solution)/shard_map/ppermute | solution.py:16
  30.7 19.0 %collective-permute-start.1 = (s32[128]{0:T(128)S(1)}, s32[128]{0:T(128)S(1)}, u32[]{:S(2)}, u32[]{:S(2)}) collective-permute-start(s32[128]{0:T(128)S(1)} %collective-permute-done), channel_id=1, source_target_pairs={{0,8},{8,16},{16,24},{1,9},{9,17},{17,25},{2,10},{10,18},{18,26},{... | collective-permute-start | bytes 1544 | tf_op jit(solution)/shard_map/ppermute | solution.py:16
  51.3 16.1 %collective-permute-start.5 = (bf16[128,2304]{1,0:T(8,128)(2,1)S(1)}, bf16[128,2304]{1,0:T(8,128)(2,1)}, u32[]{:S(2)}, u32[]{:S(2)}) collective-permute-start(bf16[128,2304]{1,0:T(8,128)(2,1)S(1)} %collective-permute-done.4), channel_id=1, source_target_pairs={{0,8},{8,16},{16,24},{1,9},{9,17},{17,25},{2,10},{10,18},{18,26},{... | collective-permute-start | bytes 1769480 | tf_op jit(solution)/shard_map/ppermute | solution.py:16
  59.1 9.7 %copy-start.1 = (bf16[1,128,2304]{1,2,0:T(8,128)(2,1)S(1)}, bf16[1,128,2304]{1,2,0:T(8,128)(2,1)}, u32[]{:S(2)}) copy-start(bf16[1,128,2304]{1,2,0:T(8,128)(2,1)} %copy.100) | copy-start | bytes 1769476
  59.1 9.7 %copy-start.2 = (bf16[128,2304]{0,1:T(8,128)(2,1)S(1)}, bf16[128,2304]{0,1:T(8,128)(2,1)}, u32[]{:S(2)}) copy-start(bf16[128,2304]{0,1:T(8,128)(2,1)} %copy.99) | copy-start | bytes 1769476
  68.9 2.9 copy-start.3
  71.8 5.8 %copy-start.4 = (f32[2304]{0:T(1024)S(1)}, f32[2304]{0:T(1024)}, u32[]{:S(2)}) copy-start(f32[2304]{0:T(1024)} %param.17) | copy-start | bytes 27652
  96.6 121.3 %all-gather.5.cloned.1.call-start = ((), (), s32[]{:S(2)}) async-start(), calls=%async_computation.8 | async-start | bytes 3686400 | tf_op jit(solution)/shard_map/all_gather | solution.py:122
  113.6 171.6 %reduce-scatter.5.cloned.1.call-start = ((), (), s32[]{:S(2)}) async-start(), calls=%async_computation.7 | async-start | bytes 4423680 | tf_op jit(solution)/shard_map/reduce_scatter | solution.py:130
  197.1 157.0 %reduce-scatter.3.cloned.1.call-start = ((), (), s32[]{:S(2)}) async-start(), calls=%async_computation.6 | async-start | bytes 4423680 | tf_op jit(solution)/shard_map/reduce_scatter | solution.py:130
  257.7 100.4 %copy-start.5 = (s32[1,128,2]{1,2,0:T(2,128)S(1)}, s32[1,128,2]{1,2,0:T(2,128)}, u32[]{:S(2)}) copy-start(s32[1,128,2]{1,2,0:T(2,128)} %param.19) | copy-start | bytes 3076
  285.3 68.8 %all-to-all-start.3 = ((bf16[8,20,2304]{2,1,0:T(8,128)(2,1)}), bf16[8,20,2304]{2,1,0:T(8,128)(2,1)S(1)}, u32[]{:S(2)}, u32[]{:S(2)}) async-start(bf16[8,20,2304]{2,1,0:T(8,128)(2,1)} %bitcast.76), calls=%async_computation.5 | async-start | bytes 1769472 | tf_op jit(solution)/shard_map/all_to_all | solution.py:132
  354.1 17.3 %all-to-all-start.1 = ((bf16[8,20,2304]{2,1,0:T(8,128)(2,1)}), bf16[8,20,2304]{2,1,0:T(8,128)(2,1)S(1)}, u32[]{:S(2)}, u32[]{:S(2)}) async-start(bf16[8,20,2304]{2,1,0:T(8,128)(2,1)} %bitcast.77), calls=%async_computation.2 | async-start | bytes 1769472 | tf_op jit(solution)/shard_map/all_to_all | solution.py:132
Sparse Core Ops, SparseCore 0:
  96.7 60.5 all-gather.6
  158.9 58.9 all-gather.4
  220.2 65.0 reduce-scatter.4
  287.4 66.6 reduce-scatter.2
